TPU v7x, 32 devices: a whole 2x2x4 slice. The times are simulated.
32 devices in a mesh: mol: 2 (over x), occ: 16 (over z, y, core).
Axes of the slice: x: 2, y: 2, z: 4, core: 2. Of those that a mesh axis runs over, the one named last changes fastest.
Arguments:
- integrals: bfloat16 [512, 128, 2048], P(('mol', 'occ')), parts along dimension 0, may hold values from -6 to 6
- orbitals: bfloat16 [4096, 1536], P('mol'), parts along dimension 0
- occ_energy: float32 [256], P('mol'), parts along dimension 0, may hold values from -2 to -0.3
- vir_energy: float32 [3072], P('mol'), parts along dimension 0, may hold values from 0.1 to 3
- owner: int32 [16], P('mol'), parts along dimension 0, may hold values from 0 to 127
- vblock: int32 [16], P('mol'), parts along dimension 0, may hold values from 0 to 7
Outputs:
- factors: bfloat16 [512, 128, 1536], P('mol', 'occ'), parts along dimension 0
- pair_energy: float32 [256, 8], P(('mol', 'occ')), parts along dimension 0
There are 2 independent parts, one for each index of `mol`. A program takes and returns all parts, laid end to end along the dimension named above; each array names one. Nothing has to cross between parts.
Inputs may be any that keep to these rules, and one draw needn't show every extreme that they name: `owner`: each step names one occupied orbital and one virtual block; steps may repeat.
All inputs are finite; a program needn't handle non-finite values.
Results may differ from a plain program's by a relative error of at most 0.001.
Values may be sent and summed in bfloat16 or wider, within the bound.
No kernel may reach another device: no remote copies, remote signals or barrier semaphores. Data moves between devices by JAX's collectives and lax.ppermute only.
A program may use at most 128 MiB of HBM per device.

v0:
```python
import jax
import jax.numpy as jnp
from jax import lax
from jax.sharding import PartitionSpec as P

VBLK = 192


def from_root(x, axis, root):
    mine = lax.axis_index(axis) == root
    return lax.psum(jnp.where(mine, x, jnp.zeros_like(x)), axis)


def pick_block(factors, orbital_j, block_id):
    local_count = factors.shape[1]
    row = orbital_j % local_count
    piece = lax.dynamic_slice(
        factors, (jnp.int32(0), row, block_id * VBLK), (factors.shape[0], 1, VBLK)
    )
    return (piece[:, 0, :], orbital_j // local_count)


def pair_column(factors, block, occ_here, occ_energy, vir_energy, orbital_j, block_id):
    coulomb = lax.dot_general(
        factors, block, (((0,), (0,)), ((), ())), preferred_element_type=jnp.float32
    )
    vir_block = lax.dynamic_slice(vir_energy, (block_id * VBLK,), (VBLK,))
    occ_j = occ_energy[orbital_j]
    denom = vir_energy[None, :, None] + vir_block[None, None, :] - occ_here[:, None, None] - occ_j
    scale = 1.0 / (factors.shape[0] * vir_energy.shape[0] * VBLK)
    return -jnp.sum(coulomb * coulomb / denom, axis=(1, 2)) * scale


def per_device(integrals, orbitals, occ_energy, vir_energy, owner, vblock):
    aux_here, occ_total, basis_count = integrals.shape
    step_count = owner.shape[0]
    flat = integrals.reshape(aux_here * occ_total, basis_count)
    product = jnp.dot(flat, orbitals, preferred_element_type=jnp.float32).astype(jnp.bfloat16)
    product = product.reshape(aux_here, occ_total, orbitals.shape[1])
    factors = lax.all_to_all(product, "occ", split_axis=1, concat_axis=0, tiled=True)
    local_count = factors.shape[1]
    occ_here = lax.dynamic_slice(occ_energy, (lax.axis_index("occ") * local_count,), (local_count,))
    energies = jnp.zeros((local_count, step_count), jnp.float32)

    def step_body(step, energies):
        orbital_j = owner[step]
        block_id = vblock[step]
        piece, root = pick_block(factors, orbital_j, block_id)
        block = from_root(piece, "occ", root)
        column = pair_column(factors, block, occ_here, occ_energy, vir_energy, orbital_j, block_id)
        return lax.dynamic_update_slice(energies, column[:, None], (jnp.int32(0), step))

    energies = lax.fori_loop(0, step_count, step_body, energies)
    return (factors, energies)


def solution(mesh):
    placed = (P(("mol", "occ"), None, None), P("mol", None), P("mol"), P("mol"), P("mol"), P("mol"))
    return jax.shard_map(
        per_device,
        mesh=mesh,
        in_specs=placed,
        out_specs=(P("mol", "occ", None), P(("mol", "occ"), None)),
        check_vma=False,
    )
```

profile of v0, /device:TPU:0, one launch (start us, length us, event | category | flops | bytes accessed | tf_op | source)
XLA Modules:
  0.0 991.6 jit_solution(14299061636335354797)
XLA Ops:
  7.2 17.3 %convolution_convert_fusion = bf16[2048,1536]{1,0:T(8,128)(2,1)S(1)} fusion(bf16[2048,2048]{1,0:T(8,128)(2,1)} %bitcast.42, bf16[2048,1536]{1,0:T(8,128)(2,1)} %param.9), kind=kOutput, calls=%fused_computation.6 | convolution fusion | flops 12888047616 | bytes 20971520 | tf_op jit(solution)/shard_map/dot_general | solution.py:38
  24.4 6.2 copy.13
  30.6 7.6 all-to-all-start
  38.3 114.1 %all-to-all-done = bf16[16,128,1536]{2,0,1:T(8,128)(2,1)} async-done(((bf16[16,128,1536]{2,0,1:T(8,128)(2,1)}), bf16[16,128,1536]{2,0,1:T(8,128)(2,1)}, u32[]{:S(2)}, u32[]{:S(2)}) %all-to-all-start) | async-done | bytes 6291488 | tf_op jit(solution)/shard_map/all_to_all | solution.py:40
  152.4 9.6 copy.14
  162.0 9.1 copy.15
  171.1 812.9 %while.15 = (s32[]{:T(128)}, f32[8,8]{0,1:T(8,128)S(1)}, s32[8]{0:T(128)S(1)}, s32[8]{0:T(128)S(1)}, bf16[256,8,1536]{0,2,1:T(8,128)(2,1)}, /*index=5*/f32[1536]...) while((s32[]{:T(128)}, f32[8,8]{0,1:T(8,128)S(1)}, ...), condition=%wide.region_3.4_spmd, body=%wide.region_0.3_spmd.sunk | while | flops 1220149248 | bytes 9544719 | solution.py:53
  175.6 1.6 select_bitcast_fusion.2
  179.3 108.6 %all-reduce.2.cloned.1.call-done = bf16[256,192]{0,1:T(8,128)(2,1)} async-done(((bf16[256,192]{0,1:T(8,128)(2,1)}), bf16[256,192]{0,1:T(8,128)(2,1)}) %all-reduce.2.cloned.1.call-update) | async-done | bytes 98320 | tf_op jit(solution)/shard_map/while/body/eval_jaxpr/psum | solution.py:11
  287.9 6.2 fusion.10
  298.6 1.6 select_bitcast_fusion.2
  302.3 84.2 %all-reduce.2.cloned.1.call-done = bf16[256,192]{0,1:T(8,128)(2,1)} async-done(((bf16[256,192]{0,1:T(8,128)(2,1)}), bf16[256,192]{0,1:T(8,128)(2,1)}) %all-reduce.2.cloned.1.call-update) | async-done | bytes 98320 | tf_op jit(solution)/shard_map/while/body/eval_jaxpr/psum | solution.py:11
  386.5 6.1 fusion.10
  397.2 1.6 select_bitcast_fusion.2
  400.9 84.2 %all-reduce.2.cloned.1.call-done = bf16[256,192]{0,1:T(8,128)(2,1)} async-done(((bf16[256,192]{0,1:T(8,128)(2,1)}), bf16[256,192]{0,1:T(8,128)(2,1)}) %all-reduce.2.cloned.1.call-update) | async-done | bytes 98320 | tf_op jit(solution)/shard_map/while/body/eval_jaxpr/psum | solution.py:11
  485.1 6.1 fusion.10
  495.7 1.6 select_bitcast_fusion.2
  499.5 84.2 %all-reduce.2.cloned.1.call-done = bf16[256,192]{0,1:T(8,128)(2,1)} async-done(((bf16[256,192]{0,1:T(8,128)(2,1)}), bf16[256,192]{0,1:T(8,128)(2,1)}) %all-reduce.2.cloned.1.call-update) | async-done | bytes 98320 | tf_op jit(solution)/shard_map/while/body/eval_jaxpr/psum | solution.py:11
  583.6 6.1 fusion.10
  594.3 1.6 select_bitcast_fusion.2
  598.0 84.2 %all-reduce.2.cloned.1.call-done = bf16[256,192]{0,1:T(8,128)(2,1)} async-done(((bf16[256,192]{0,1:T(8,128)(2,1)}), bf16[256,192]{0,1:T(8,128)(2,1)}) %all-reduce.2.cloned.1.call-update) | async-done | bytes 98320 | tf_op jit(solution)/shard_map/while/body/eval_jaxpr/psum | solution.py:11
  682.2 6.1 fusion.10
  692.9 1.6 select_bitcast_fusion.2
  696.6 84.2 %all-reduce.2.cloned.1.call-done = bf16[256,192]{0,1:T(8,128)(2,1)} async-done(((bf16[256,192]{0,1:T(8,128)(2,1)}), bf16[256,192]{0,1:T(8,128)(2,1)}) %all-reduce.2.cloned.1.call-update) | async-done | bytes 98320 | tf_op jit(solution)/shard_map/while/body/eval_jaxpr/psum | solution.py:11
  780.8 6.1 fusion.10
  791.4 1.6 select_bitcast_fusion.2
  795.1 84.2 %all-reduce.2.cloned.1.call-done = bf16[256,192]{0,1:T(8,128)(2,1)} async-done(((bf16[256,192]{0,1:T(8,128)(2,1)}), bf16[256,192]{0,1:T(8,128)(2,1)}) %all-reduce.2.cloned.1.call-update) | async-done | bytes 98320 | tf_op jit(solution)/shard_map/while/body/eval_jaxpr/psum | solution.py:11
  879.3 6.1 fusion.10
  890.0 1.6 select_bitcast_fusion.2
  893.7 84.2 %all-reduce.2.cloned.1.call-done = bf16[256,192]{0,1:T(8,128)(2,1)} async-done(((bf16[256,192]{0,1:T(8,128)(2,1)}), bf16[256,192]{0,1:T(8,128)(2,1)}) %all-reduce.2.cloned.1.call-update) | async-done | bytes 98320 | tf_op jit(solution)/shard_map/while/body/eval_jaxpr/psum | solution.py:11
  977.9 6.1 fusion.10
  984.1 0.7 copy.16
  (82 shorter events, 17.7 us)
Async XLA Ops:
  30.6 7.6 copy-start.3
  30.6 121.8 %all-to-all-start = ((bf16[16,128,1536]{2,0,1:T(8,128)(2,1)}), bf16[16,128,1536]{2,0,1:T(8,128)(2,1)}, u32[]{:S(2)}, u32[]{:S(2)}) async-start(bf16[16,128,1536]{2,0,1:T(8,128)(2,1)} %copy.13), calls=%async_computation | async-start | bytes 12582912 | tf_op jit(solution)/shard_map/all_to_all | solution.py:40
  162.0 9.1 copy-start
  162.0 9.1 copy-start.1
  162.0 9.1 copy-start.2
  171.2 116.8 %all-reduce.2.cloned.1.call-start = ((), (), s32[]{:S(2)}) async-start(), calls=%async_computation.1 | async-start | bytes 196608 | tf_op jit(solution)/shard_map/while/body/eval_jaxpr/psum | solution.py:11
  294.1 92.4 %all-reduce.2.cloned.1.call-start = ((), (), s32[]{:S(2)}) async-start(), calls=%async_computation.1 | async-start | bytes 196608 | tf_op jit(solution)/shard_map/while/body/eval_jaxpr/psum | solution.py:11
  392.7 92.4 %all-reduce.2.cloned.1.call-start = ((), (), s32[]{:S(2)}) async-start(), calls=%async_computation.1 | async-start | bytes 196608 | tf_op jit(solution)/shard_map/while/body/eval_jaxpr/psum | solution.py:11
  491.3 92.4 %all-reduce.2.cloned.1.call-start = ((), (), s32[]{:S(2)}) async-start(), calls=%async_computation.1 | async-start | bytes 196608 | tf_op jit(solution)/shard_map/while/body/eval_jaxpr/psum | solution.py:11
  589.8 92.4 %all-reduce.2.cloned.1.call-start = ((), (), s32[]{:S(2)}) async-start(), calls=%async_computation.1 | async-start | bytes 196608 | tf_op jit(solution)/shard_map/while/body/eval_jaxpr/psum | solution.py:11
  688.4 92.4 %all-reduce.2.cloned.1.call-start = ((), (), s32[]{:S(2)}) async-start(), calls=%async_computation.1 | async-start | bytes 196608 | tf_op jit(solution)/shard_map/while/body/eval_jaxpr/psum | solution.py:11
  787.0 92.4 %all-reduce.2.cloned.1.call-start = ((), (), s32[]{:S(2)}) async-start(), calls=%async_computation.1 | async-start | bytes 196608 | tf_op jit(solution)/shard_map/while/body/eval_jaxpr/psum | solution.py:11
  885.5 92.4 %all-reduce.2.cloned.1.call-start = ((), (), s32[]{:S(2)}) async-start(), calls=%async_computation.1 | async-start | bytes 196608 | tf_op jit(solution)/shard_map/while/body/eval_jaxpr/psum | solution.py:11
Sparse Core Ops, SparseCore 0:
  177.3 110.5 all-reduce.1
  300.3 86.1 all-reduce.1
  398.9 86.1 all-reduce.1
  497.5 86.1 all-reduce.1
  596.0 86.1 all-reduce.1
  694.6 86.1 all-reduce.1
  793.1 86.1 all-reduce.1
  891.7 86.1 all-reduce.1
where the time goes:
time: 993 us; the launch traced here: 992 us
  waiting for transfers between devices  812 us (82%)
  matrix products  66.4 us (7%)
  local copies, waits for them, and re-layouts  41.6 us (4%)
  loops' own time  35.7 us (4%)
  between operations  14.1 us (1%)
  other arithmetic  13.8 us (1%)
    psum x8, waiting for transfers between devices, from_root(): return lax.psum(jnp.where(mine, x, jnp.zeros_like(x)), axis)  698 us
    all_to_all x1, waiting for transfers between devices, per_device(): lax.all_to_all(product, 'occ', split_axis=1, concat_axis=0, tiled=True)  114 us
    dot_general x8, matrix products, pair_column(): lax.dot_general(factors, block, (((0,), (0,)), ((), ())), preferred_eleme...  49.2 us
    another operation x1, loops' own time, per_device(): energies = lax.fori_loop(0, step_count, step_body, energies)  35.7 us
  transfers between devices with their start and end apart: 9, of which 9 were waited for; matrix products, arithmetic and copies ran while one was open for 1% of the time, Pallas kernels for 0%

commit v1 on v0

--- a/solution.py
+++ b/solution.py
@@ -37,7 +37,11 @@
     flat = integrals.reshape(aux_here * occ_total, basis_count)
     product = jnp.dot(flat, orbitals, preferred_element_type=jnp.float32).astype(jnp.bfloat16)
     product = product.reshape(aux_here, occ_total, orbitals.shape[1])
-    factors = lax.all_to_all(product, "occ", split_axis=1, concat_axis=0, tiled=True)
+    work_now = lax.axis_size("occ")
+    mixed_arr = jnp.split(product, work_now, axis=1)
+    outcome_arr = jnp.stack(mixed_arr, axis=0)
+    p_next = lax.all_to_all(outcome_arr, "occ", 0, 0)
+    factors = jnp.concatenate(p_next, axis=0)
     local_count = factors.shape[1]
     occ_here = lax.dynamic_slice(occ_energy, (lax.axis_index("occ") * local_count,), (local_count,))
     energies = jnp.zeros((local_count, step_count), jnp.float32)

time: 993 us -> 995 us (level)
    unnamed x9 -> x25, local copies, waits for them, and re-layouts: 0.68 us -> 18.2 us
where the time goes in v1:
time: 995 us; the launch traced here: 994 us
  waiting for transfers between devices  812 us (82%)
  matrix products  66.4 us (7%)
  local copies, waits for them, and re-layouts  44.1 us (4%)
  loops' own time  35.7 us (4%)
  between operations  14.1 us (1%)
  other arithmetic  13.8 us (1%)
    psum x8, waiting for transfers between devices, from_root(): return lax.psum(jnp.where(mine, x, jnp.zeros_like(x)), axis)  698 us
    all_to_all x1, waiting for transfers between devices, per_device(): p_next = lax.all_to_all(outcome_arr, 'occ', 0, 0)  114 us
    dot_general x8, matrix products, pair_column(): lax.dot_general(factors, block, (((0,), (0,)), ((), ())), preferred_eleme...  49.2 us
    another operation x1, loops' own time, per_device(): energies = lax.fori_loop(0, step_count, step_body, energies)  35.7 us
  transfers between devices with their start and end apart: 9, of which 9 were waited for; matrix products, arithmetic and copies ran while one was open for 1% of the time, Pallas kernels for 0%

profile of v1, /device:TPU:0, one launch (start us, length us, event | category | flops | bytes accessed | tf_op | source)
XLA Modules:
  0.0 994.1 jit_solution(7420790037926338550)
XLA Ops:
  7.2 17.3 %convolution_convert_fusion = bf16[2048,1536]{1,0:T(8,128)(2,1)S(1)} fusion(bf16[2048,2048]{1,0:T(8,128)(2,1)} %bitcast.116, bf16[2048,1536]{1,0:T(8,128)(2,1)} %param.9), kind=kOutput, calls=%fused_computation.6 | convolution fusion | flops 12888047616 | bytes 20971520 | tf_op jit(solution)/shard_map/dot_general | solution.py:38
  26.0 0.8 fusion.15
  28.3 0.8 fusion.12
  36.8 7.6 all-to-all-start
  44.5 114.1 %all-to-all-done = bf16[16,16,8,1536]{3,2,1,0:T(8,128)(2,1)} async-done(((bf16[16,16,8,1536]{3,2,1,0:T(8,128)(2,1)}), bf16[16,16,8,1536]{3,2,1,0:T(8,128)(2,1)}, u32[]{:S(2)}, u32[]{:S(2)}) %all-to-all-start) | async-done | bytes 6291488 | tf_op jit(solution)/shard_map/all_to_all | solution.py:43
  158.6 9.1 copy.9
  167.7 813.0 %while.15 = (s32[]{:T(128)}, f32[8,8]{0,1:T(8,128)S(1)}, s32[8]{0:T(128)S(1)}, s32[8]{0:T(128)S(1)}, bf16[256,8,1536]{0,2,1:T(8,128)(2,1)}, /*index=5*/f32[1536]...) while((s32[]{:T(128)}, f32[8,8]{0,1:T(8,128)S(1)}, ...), condition=%wide.region_3.4_spmd, body=%wide.region_0.3_spmd.sunk | while | flops 1220149248 | bytes 9544719 | solution.py:57
  172.2 1.6 select_bitcast_fusion.2
  175.9 108.6 %all-reduce.2.cloned.1.call-done = bf16[256,192]{0,1:T(8,128)(2,1)} async-done(((bf16[256,192]{0,1:T(8,128)(2,1)}), bf16[256,192]{0,1:T(8,128)(2,1)}) %all-reduce.2.cloned.1.call-update) | async-done | bytes 98320 | tf_op jit(solution)/shard_map/while/body/eval_jaxpr/psum | solution.py:11
  284.5 6.1 fusion.26
  295.1 1.6 select_bitcast_fusion.2
  298.8 84.2 %all-reduce.2.cloned.1.call-done = bf16[256,192]{0,1:T(8,128)(2,1)} async-done(((bf16[256,192]{0,1:T(8,128)(2,1)}), bf16[256,192]{0,1:T(8,128)(2,1)}) %all-reduce.2.cloned.1.call-update) | async-done | bytes 98320 | tf_op jit(solution)/shard_map/while/body/eval_jaxpr/psum | solution.py:11
  383.0 6.1 fusion.26
  393.7 1.6 select_bitcast_fusion.2
  397.4 84.2 %all-reduce.2.cloned.1.call-done = bf16[256,192]{0,1:T(8,128)(2,1)} async-done(((bf16[256,192]{0,1:T(8,128)(2,1)}), bf16[256,192]{0,1:T(8,128)(2,1)}) %all-reduce.2.cloned.1.call-update) | async-done | bytes 98320 | tf_op jit(solution)/shard_map/while/body/eval_jaxpr/psum | solution.py:11
  481.6 6.1 fusion.26
  492.3 1.6 select_bitcast_fusion.2
  496.0 84.2 %all-reduce.2.cloned.1.call-done = bf16[256,192]{0,1:T(8,128)(2,1)} async-done(((bf16[256,192]{0,1:T(8,128)(2,1)}), bf16[256,192]{0,1:T(8,128)(2,1)}) %all-reduce.2.cloned.1.call-update) | async-done | bytes 98320 | tf_op jit(solution)/shard_map/while/body/eval_jaxpr/psum | solution.py:11
  580.2 6.1 fusion.26
  590.9 1.6 select_bitcast_fusion.2
  594.6 84.2 %all-reduce.2.cloned.1.call-done = bf16[256,192]{0,1:T(8,128)(2,1)} async-done(((bf16[256,192]{0,1:T(8,128)(2,1)}), bf16[256,192]{0,1:T(8,128)(2,1)}) %all-reduce.2.cloned.1.call-update) | async-done | bytes 98320 | tf_op jit(solution)/shard_map/while/body/eval_jaxpr/psum | solution.py:11
  678.8 6.1 fusion.26
  689.5 1.6 select_bitcast_fusion.2
  693.2 84.2 %all-reduce.2.cloned.1.call-done = bf16[256,192]{0,1:T(8,128)(2,1)} async-done(((bf16[256,192]{0,1:T(8,128)(2,1)}), bf16[256,192]{0,1:T(8,128)(2,1)}) %all-reduce.2.cloned.1.call-update) | async-done | bytes 98320 | tf_op jit(solution)/shard_map/while/body/eval_jaxpr/psum | solution.py:11
  777.4 6.1 fusion.26
  788.0 1.6 select_bitcast_fusion.2
  791.8 84.2 %all-reduce.2.cloned.1.call-done = bf16[256,192]{0,1:T(8,128)(2,1)} async-done(((bf16[256,192]{0,1:T(8,128)(2,1)}), bf16[256,192]{0,1:T(8,128)(2,1)}) %all-reduce.2.cloned.1.call-update) | async-done | bytes 98320 | tf_op jit(solution)/shard_map/while/body/eval_jaxpr/psum | solution.py:11
  876.0 6.1 fusion.26
  886.6 1.6 select_bitcast_fusion.2
  890.3 84.2 %all-reduce.2.cloned.1.call-done = bf16[256,192]{0,1:T(8,128)(2,1)} async-done(((bf16[256,192]{0,1:T(8,128)(2,1)}), bf16[256,192]{0,1:T(8,128)(2,1)}) %all-reduce.2.cloned.1.call-update) | async-done | bytes 98320 | tf_op jit(solution)/shard_map/while/body/eval_jaxpr/psum | solution.py:11
  974.6 6.1 fusion.26
  981.4 5.9 copy.36
  (97 shorter events, 29.2 us)
Async XLA Ops:
  36.8 7.6 copy-start.3
  36.8 121.8 %all-to-all-start = ((bf16[16,16,8,1536]{3,2,1,0:T(8,128)(2,1)}), bf16[16,16,8,1536]{3,2,1,0:T(8,128)(2,1)}, u32[]{:S(2)}, u32[]{:S(2)}) async-start(bf16[16,16,8,1536]{3,2,1,0:T(8,128)(2,1)} %fusion.2), calls=%async_computation | async-start | bytes 12582912 | tf_op jit(solution)/shard_map/all_to_all | solution.py:43
  158.6 9.1 copy-start
  158.6 9.1 copy-start.1
  158.6 9.1 copy-start.2
  167.7 116.8 %all-reduce.2.cloned.1.call-start = ((), (), s32[]{:S(2)}) async-start(), calls=%async_computation.1 | async-start | bytes 196608 | tf_op jit(solution)/shard_map/while/body/eval_jaxpr/psum | solution.py:11
  290.6 92.4 %all-reduce.2.cloned.1.call-start = ((), (), s32[]{:S(2)}) async-start(), calls=%async_computation.1 | async-start | bytes 196608 | tf_op jit(solution)/shard_map/while/body/eval_jaxpr/psum | solution.py:11
  389.2 92.4 %all-reduce.2.cloned.1.call-start = ((), (), s32[]{:S(2)}) async-start(), calls=%async_computation.1 | async-start | bytes 196608 | tf_op jit(solution)/shard_map/while/body/eval_jaxpr/psum | solution.py:11
  487.8 92.4 %all-reduce.2.cloned.1.call-start = ((), (), s32[]{:S(2)}) async-start(), calls=%async_computation.1 | async-start | bytes 196608 | tf_op jit(solution)/shard_map/while/body/eval_jaxpr/psum | solution.py:11
  586.4 92.4 %all-reduce.2.cloned.1.call-start = ((), (), s32[]{:S(2)}) async-start(), calls=%async_computation.1 | async-start | bytes 196608 | tf_op jit(solution)/shard_map/while/body/eval_jaxpr/psum | solution.py:11
  685.0 92.4 %all-reduce.2.cloned.1.call-start = ((), (), s32[]{:S(2)}) async-start(), calls=%async_computation.1 | async-start | bytes 196608 | tf_op jit(solution)/shard_map/while/body/eval_jaxpr/psum | solution.py:11
  783.6 92.4 %all-reduce.2.cloned.1.call-start = ((), (), s32[]{:S(2)}) async-start(), calls=%async_computation.1 | async-start | bytes 196608 | tf_op jit(solution)/shard_map/while/body/eval_jaxpr/psum | solution.py:11
  882.2 92.4 %all-reduce.2.cloned.1.call-start = ((), (), s32[]{:S(2)}) async-start(), calls=%async_computation.1 | async-start | bytes 196608 | tf_op jit(solution)/shard_map/while/body/eval_jaxpr/psum | solution.py:11
Sparse Core Ops, SparseCore 0:
  173.9 110.5 all-reduce.1
  296.8 86.1 all-reduce.1
  395.4 86.1 all-reduce.1
  494.0 86.1 all-reduce.1
  592.6 86.1 all-reduce.1
  691.2 86.1 all-reduce.1
  789.8 86.1 all-reduce.1
  888.3 86.1 all-reduce.1
